TPU v7x, 32 devices: a whole 2x2x4 slice. The times are simulated.
32 devices in a mesh: ctx: 4 (over z), row: 8 (over y, x, core).
Axes of the slice: x: 2, y: 2, z: 4, core: 2. Of those that a mesh axis runs over, the one named last changes fastest.
Arguments:
- queries: bfloat16 [2048, 2048], P('row'), may hold values from -120 to 120
- keys: bfloat16 [1536, 2048], P('ctx'), may hold values from -5 to 5
- values: bfloat16 [1536, 2048], P('ctx'), may hold values from -6 to 6
- block_list: int32 [16, 8], P('row'), may hold values from 0 to 11, as said below
- block_count: int32 [16], P('row'), may hold values from 1 to 8, as said below
Outputs:
- owned: bfloat16 [2048, 2048], P('row', 'ctx')
Inputs may be any that keep to these rules, and one draw needn't show every extreme that they name: `block_list`: entries of one list are distinct; the first entry of the list of query block b is b % 12. Entries past block_count are ignored. `block_count`: every query block uses at least one list entry.
All inputs are finite; a program needn't handle non-finite values.
Results may differ from a plain program's by a relative error of at most 0.0044.
Values may be sent and summed in bfloat16 or wider, within the bound.
No kernel may reach another device: no remote copies, remote signals or barrier semaphores. Data moves between devices by JAX's collectives and lax.ppermute only.
A program may use at most 64 MiB of HBM per device.

v0:
```python
import jax
import jax.numpy as jnp
from jax import lax
from jax.sharding import PartitionSpec as P

HEADS = 16
HEAD_DIM = 128
BLOCK = 128
masked_fill = -1e30


def combine_rows(pieces):
    maxima, totals, partial_out = pieces
    item_rows, sources, head_share = maxima.shape
    row_best = jnp.max(maxima, axis=1)
    weight = jnp.exp(maxima - row_best[:, None, :])
    total_sum = jnp.sum(totals * weight, axis=1)
    out_heads = partial_out.reshape(item_rows, sources, head_share, HEAD_DIM)
    numerator = jnp.sum(out_heads * weight[:, :, :, None], axis=1)
    return (numerator / total_sum[:, :, None]).reshape(item_rows, head_share * HEAD_DIM)


def chosen_range(block_list, block_count, first_block, block_span):
    slot_live = jnp.arange(block_list.shape[1], dtype=jnp.int32)[None, :] < block_count[:, None]
    block_ids = first_block + jnp.arange(block_span, dtype=jnp.int32)
    block_hits = (block_list[:, :, None] == block_ids[None, None, :]) & slot_live[:, :, None]
    return jnp.any(block_hits, axis=1)


def segment_parts(query_heads, key_heads, value_heads, chosen):
    key_live = jnp.repeat(jnp.repeat(chosen, BLOCK, axis=0), BLOCK, axis=1)[None, :, :]
    score_scale = 1.0 / HEAD_DIM**0.5
    scores = (
        jnp.einsum("qhd,khd->hqk", query_heads, key_heads, preferred_element_type=jnp.float32)
        * score_scale
    )
    seg_max = jnp.max(jnp.where(key_live, scores, masked_fill), axis=2)
    probs_live = jnp.where(key_live, jnp.exp(scores - seg_max[:, :, None]), 0.0)
    seg_total = jnp.sum(probs_live, axis=2)
    probs_low = probs_live.astype(jnp.bfloat16)
    seg_out = jnp.einsum("hqk,khd->qhd", probs_low, value_heads, preferred_element_type=jnp.float32)
    return (seg_max, seg_total, seg_out)


def local_parts(queries, keys, values, block_list, block_count):
    row_count = queries.shape[0]
    ctx_span = keys.shape[0]
    blocks_here = ctx_span // BLOCK
    chosen = chosen_range(block_list, block_count, lax.axis_index("ctx") * blocks_here, blocks_here)
    return segment_parts(
        queries.reshape(row_count, HEADS, HEAD_DIM),
        keys.reshape(ctx_span, HEADS, HEAD_DIM),
        values.reshape(ctx_span, HEADS, HEAD_DIM),
        chosen,
    )


def local(queries, keys, values, block_list, block_count):
    row_count = queries.shape[0]
    shards = lax.axis_size("ctx")
    head_share = HEADS // shards
    share_width = head_share * HEAD_DIM
    seg_max, seg_total, seg_out = local_parts(queries, keys, values, block_list, block_count)
    sent = (
        jnp.transpose(seg_max)[:, None, :],
        jnp.transpose(seg_total)[:, None, :],
        seg_out.reshape(row_count, 1, HEADS * HEAD_DIM),
    )
    attended = combine_rows(
        (
            lax.all_to_all(sent[0], "ctx", split_axis=2, concat_axis=1, tiled=True),
            lax.all_to_all(sent[1], "ctx", split_axis=2, concat_axis=1, tiled=True),
            lax.all_to_all(sent[2], "ctx", split_axis=2, concat_axis=1, tiled=True),
        )
    )
    attended_low = attended.astype(jnp.bfloat16)
    owners = lax.axis_size("row")
    per_owner = row_count // owners
    grouped = attended_low.reshape(per_owner, owners, share_width)
    regrouped = lax.all_to_all(grouped, "row", split_axis=1, concat_axis=0, tiled=True)
    return regrouped.reshape(row_count, share_width)


def solution(mesh):
    return jax.shard_map(
        local,
        mesh=mesh,
        in_specs=(P("row", None), P("ctx", None), P("ctx", None), P("row", None), P("row")),
        out_specs=P("row", "ctx"),
        check_vma=False,
    )
```

profile of v0, /device:TPU:0, one launch (start us, length us, event | category | flops | bytes accessed | tf_op | source)
XLA Modules:
  0.0 105.7 jit_solution(18359404160349722766)
XLA Ops:
  0.0 0.0 copy-start
  0.0 0.8 iota_compare_fusion
  0.9 0.9 and_reduce_fusion
  1.7 0.1 broadcast_bitcast_fusion
  1.8 0.2 copy.27
  2.0 0.0 copy-done
  2.0 5.2 %select_reduce_fusion = (f32[16,256]{1,0:T(8,128)S(1)}, f32[16,256,384]{2,1,0:T(8,128)}) fusion(pred[256,384]{1,0:T(8,128)(4,1)S(1)} %copy.27, bf16[384,2048]{1,0:T(8,128)(2,1)S(1)} %copy-done, bf16[256,2048]{1,0:T(8,128)(2,1)} %param.5), kind=kOutput, calls=%fused_computation.1 | convolution fusion | flops 407367680 | bytes 9027584 | tf_op jit(solution)/shard_map/qhd,khd->hqk/dot_general | solution.py:34
  7.2 0.6 broadcast_in_dim.47
  7.9 6.3 %all-to-all-start.1 = ((f32[256,1,16]{0,1,2:T(1,128)}), f32[256,1,16]{0,1,2:T(1,128)S(1)}, u32[]{:S(2)}, u32[]{:S(2)}) async-start(f32[256,1,16]{0,1,2:T(1,128)} %broadcast_in_dim.47), calls=%async_computation.1 | async-start | bytes 32768 | tf_op jit(solution)/shard_map/all_to_all | solution.py:71
  14.2 0.0 copy-start.1
  14.2 4.0 %fusion = f32[16,256]{1,0:T(8,128)S(1)} fusion(f32[16,256,384]{2,1,0:T(8,128)} %get-tuple-element.8, f32[16,256]{1,0:T(8,128)S(1)} %get-tuple-element.7, pred[256,384]{1,0:T(8,128)(4,1)S(1)} %copy.27), kind=kLoop, calls=%fused_computation.2 | loop fusion | flops 6287360 | bytes 6422528 | tf_op jit(solution)/shard_map/reduce_sum | solution.py:39
  18.1 0.0 copy-done.1
  18.2 1.6 %copy.36 = bf16[384,2048]{0,1:T(8,128)(2,1)} copy(bf16[384,2048]{1,0:T(8,128)(2,1)S(1)} %copy-done.1) | data formatting | bytes 3145728 | tf_op jit(solution)/shard_map/reshape | solution.py:53
  19.7 0.6 broadcast_in_dim.48
  20.3 0.0 all-to-all-done.1
  20.3 5.1 %all-to-all-start.2 = ((f32[256,1,16]{0,1,2:T(1,128)}), f32[256,1,16]{0,1,2:T(1,128)S(1)}, u32[]{:S(2)}, u32[]{:S(2)}) async-start(f32[256,1,16]{0,1,2:T(1,128)} %broadcast_in_dim.48), calls=%async_computation.2 | async-start | bytes 32768 | tf_op jit(solution)/shard_map/all_to_all | solution.py:72
  25.4 4.2 %fusion.2 = f32[16,256,128]{1,2,0:T(8,128)S(1)} fusion(bf16[384,16,128]{0,2,1:T(8,128)(2,1)} %bitcast.49, f32[16,256,384]{2,1,0:T(8,128)} %get-tuple-element.8, f32[16,256]{1,0:T(8,128)S(1)} %get-tuple-element.7, pred[256,384]{1,0:T(8,128)(4,1)S(1)} %copy.27), kind=kOutput, calls=%fused_computation.4 | convolution fusion | flops 408944640 | bytes 10076160 | tf_op jit(solution)/shard_map/hqk,khd->qhd/dot_general | solution.py:41
  29.6 10.0 %copy.31 = f32[256,1,2048]{0,1,2:T(1,128)} copy(f32[256,1,2048]{0,2,1:T(8,128)S(1)} %bitcast.48) | data formatting | bytes 4194304 | tf_op jit(solution)/shard_map/reshape | solution.py:67
  39.6 0.0 all-to-all-done.2
  39.6 5.1 %all-to-all-start = ((f32[256,1,2048]{0,1,2:T(1,128)}), f32[256,1,2048]{0,1,2:T(1,128)}, u32[]{:S(2)}, u32[]{:S(2)}) async-start(f32[256,1,2048]{0,1,2:T(1,128)} %copy.31), calls=%async_computation | async-start | bytes 4194304 | tf_op jit(solution)/shard_map/all_to_all | solution.py:73
  44.9 0.1 copy.34
  45.0 0.3 div.12
  45.4 0.2 div.13
  45.6 46.3 %all-to-all-done = f32[256,1,2048]{0,1,2:T(1,128)} async-done(((f32[256,1,2048]{0,1,2:T(1,128)}), f32[256,1,2048]{0,1,2:T(1,128)}, u32[]{:S(2)}, u32[]{:S(2)}) %all-to-all-start) | async-done | bytes 2097184 | tf_op jit(solution)/shard_map/all_to_all | solution.py:73
  91.9 0.2 mul.38
  92.1 2.0 %fusion.8 = f32[256,512]{0,1:T(8,128)S(1)} fusion(f32[256,1,4,512]{0,3,2,1:T(8,128)S(1)} %bitcast.47, f32[256,1,4,512]{0,1,3,2:T(1,128)} %bitcast.5), kind=kLoop, calls=%fused_computation.10 | loop fusion | flops 917504 | bytes 4718592 | tf_op jit(solution)/shard_map/reduce_sum | solution.py:19
  94.1 0.2 copy.33
  94.3 0.1 fusion.14
  94.4 0.1 copy.35
  94.5 10.5 %all_to_all.51 = bf16[32,8,512]{2,0,1:T(8,128)(2,1)S(1)} all-to-all(bf16[32,8,512]{2,0,1:T(8,128)(2,1)S(1)} %copy.35), channel_id=1, replica_groups=mesh['ctx'=4,'row'=8] {'row'}, dimensions={1} | all-to-all | bytes 524288 | tf_op jit(solution)/shard_map/all_to_all | solution.py:80
  105.0 0.7 copy.57
  (8 shorter events, 0.2 us)
Async XLA Ops:
  0.0 2.0 %copy-start = (bf16[384,2048]{1,0:T(8,128)(2,1)S(1)}, bf16[384,2048]{1,0:T(8,128)(2,1)}, u32[]{:S(2)}) copy-start(bf16[384,2048]{1,0:T(8,128)(2,1)} %param.6) | copy-start | bytes 4718596
  7.9 12.5 %all-to-all-start.1 = ((f32[256,1,16]{0,1,2:T(1,128)}), f32[256,1,16]{0,1,2:T(1,128)S(1)}, u32[]{:S(2)}, u32[]{:S(2)}) async-start(f32[256,1,16]{0,1,2:T(1,128)} %broadcast_in_dim.47), calls=%async_computation.1 | async-start | bytes 32768 | tf_op jit(solution)/shard_map/all_to_all | solution.py:71
  14.2 4.0 %copy-start.1 = (bf16[384,2048]{1,0:T(8,128)(2,1)S(1)}, bf16[384,2048]{1,0:T(8,128)(2,1)}, u32[]{:S(2)}) copy-start(bf16[384,2048]{1,0:T(8,128)(2,1)} %param.7) | copy-start | bytes 4718596
  20.3 19.3 %all-to-all-start.2 = ((f32[256,1,16]{0,1,2:T(1,128)}), f32[256,1,16]{0,1,2:T(1,128)S(1)}, u32[]{:S(2)}, u32[]{:S(2)}) async-start(f32[256,1,16]{0,1,2:T(1,128)} %broadcast_in_dim.48), calls=%async_computation.2 | async-start | bytes 32768 | tf_op jit(solution)/shard_map/all_to_all | solution.py:72
  39.6 52.3 %all-to-all-start = ((f32[256,1,2048]{0,1,2:T(1,128)}), f32[256,1,2048]{0,1,2:T(1,128)}, u32[]{:S(2)}, u32[]{:S(2)}) async-start(f32[256,1,2048]{0,1,2:T(1,128)} %copy.31), calls=%async_computation | async-start | bytes 4194304 | tf_op jit(solution)/shard_map/all_to_all | solution.py:73
where the time goes:
time: 106 us
  waiting for transfers between devices  46.3 us (44%)
  starting transfers between devices  16.5 us (16%)
  local copies, waits for them, and re-layouts  15 us (14%)
  blocking collectives  10.5 us (10%)
  matrix products  9.4 us (9%)
  other arithmetic  7.93 us (7%)
    all_to_all x1, waiting for transfers between devices, local(): lax.all_to_all(sent[2], 'ctx', split_axis=2, concat_axis=1, tiled=True)  46.3 us
    all_to_all x1, blocking collectives, local(): lax.all_to_all(grouped, 'row', split_axis=1, concat_axis=0, tiled=True)  10.5 us
    reshape x1, local copies, waits for them, and re-layouts, local(): seg_out.reshape(row_count, 1, HEADS * HEAD_DIM)  10 us
    all_to_all x1, starting transfers between devices, local(): lax.all_to_all(sent[0], 'ctx', split_axis=2, concat_axis=1, tiled=True)  6.32 us
    dot_general x1, matrix products, segment_parts(): jnp.einsum('qhd,khd->hqk', query_heads, key_heads, preferred_element_type...  5.2 us
    all_to_all x1, starting transfers between devices, local(): lax.all_to_all(sent[2], 'ctx', split_axis=2, concat_axis=1, tiled=True)  5.09 us
    all_to_all x1, starting transfers between devices, local(): lax.all_to_all(sent[1], 'ctx', split_axis=2, concat_axis=1, tiled=True)  5.09 us
    dot_general x1, matrix products, segment_parts(): jnp.einsum('hqk,khd->qhd', probs_low, value_heads, preferred_element_type...  4.2 us
  transfers between devices with their start and end apart: 3, of which 1 were waited for; matrix products, arithmetic and copies ran while one was open for 20% of the time, Pallas kernels for 0%

commit v1 on v0

--- a/solution.py
+++ b/solution.py
@@ -7,6 +7,28 @@
 HEAD_DIM = 128
 BLOCK = 128
 masked_fill = -1e30
+
+
+def split_up(shard, dim, peers):
+    before, after = (shard.shape[:dim], shard.shape[dim + 1 :])
+    return jnp.moveaxis(shard.reshape(*before, peers, -1, *after), dim, 0)
+
+
+def in_order(tiles, dim):
+    shape = list(tiles.shape[1:])
+    shape[dim] *= tiles.shape[0]
+    return jnp.moveaxis(tiles, 0, dim).reshape(shape)
+
+
+def swapped_with_each(array, axis, split_dim, concat_dim):
+    length, here = (lax.axis_size(axis), lax.axis_index(axis))
+    parts = split_up(array, split_dim, length)
+    done = [parts[here]]
+    for step in range(1, length):
+        sent = parts[here ^ step]
+        done.append(lax.ppermute(sent, axis, [(i, i ^ step) for i in range(length)]))
+    parts = jnp.stack(done)[here ^ jnp.arange(length)]
+    return in_order(parts, concat_dim)
 
 
 def combine_rows(pieces):
@@ -70,7 +92,7 @@
         (
             lax.all_to_all(sent[0], "ctx", split_axis=2, concat_axis=1, tiled=True),
             lax.all_to_all(sent[1], "ctx", split_axis=2, concat_axis=1, tiled=True),
-            lax.all_to_all(sent[2], "ctx", split_axis=2, concat_axis=1, tiled=True),
+            swapped_with_each(sent[2], "ctx", 2, 1),
         )
     )
     attended_low = attended.astype(jnp.bfloat16)

time: 106 us -> 91.4 us (0.86)
  waiting for transfers between devices: 46.3 us -> 36.6 us
  local copies, waits for them, and re-layouts: 15 us -> 9.6 us
    all_to_all x1 -> x0, waiting for transfers between devices: 46.3 us -> none  [local(): lax.all_to_all(sent[2], 'ctx', split_axis=2, concat_axis=1, tiled=True)]
    all_to_all x1, waiting for transfers between devices: 0.01 us -> 36.6 us  [local(): lax.all_to_all(sent[1], 'ctx', split_axis=2, concat_axis=1, tiled=True)]
    reshape x1 -> x0, local copies, waits for them, and re-layouts: 10 us -> none  [local(): seg_out.reshape(row_count, 1, HEADS * HEAD_DIM)]
    all_to_all x1 -> x0, starting transfers between devices: 5.09 us -> none  [local(): lax.all_to_all(sent[2], 'ctx', split_axis=2, concat_axis=1, tiled=True)]
    ppermute x0 -> x3, starting transfers between devices: none -> 4.39 us  [swapped_with_each(): lax.ppermute(sent, axis, [(i, i ^ step) for i in range(length)])]
    gather x0 -> x1, local copies, waits for them, and re-layouts: none -> 3.56 us  [swapped_with_each(): parts = jnp.stack(done)[here ^ jnp.arange(length)]]
    another operation x0 -> x1, other arithmetic: none -> 2.88 us  [swapped_with_each(): parts = jnp.stack(done)[here ^ jnp.arange(length)]]
    reduce_sum x1, other arithmetic: 3.96 us -> 2.02 us  [segment_parts(): seg_total = jnp.sum(probs_live, axis=2)]
  transfers between devices with their start and end apart: 3 -> 5, of which waited for: 1 -> 1; matrix products, arithmetic and copies ran while one was open for 20% -> 12% of each run, Pallas kernels for 0% -> 0%
where the time goes in v1:
time: 91.4 us; the launch traced here: 90.9 us
  waiting for transfers between devices  36.6 us (40%)
  starting transfers between devices  15.8 us (17%)
  blocking collectives  10.5 us (11%)
  matrix products  9.65 us (11%)
  local copies, waits for them, and re-layouts  9.6 us (11%)
  other arithmetic  8.64 us (9%)
    all_to_all x1, waiting for transfers between devices, local(): lax.all_to_all(sent[1], 'ctx', split_axis=2, concat_axis=1, tiled=True)  36.6 us
    all_to_all x1, blocking collectives, local(): lax.all_to_all(grouped, 'row', split_axis=1, concat_axis=0, tiled=True)  10.5 us
    all_to_all x1, starting transfers between devices, local(): lax.all_to_all(sent[0], 'ctx', split_axis=2, concat_axis=1, tiled=True)  6.32 us
    dot_general x1, matrix products, segment_parts(): jnp.einsum('qhd,khd->hqk', query_heads, key_heads, preferred_element_type...  5.32 us
    all_to_all x1, starting transfers between devices, local(): lax.all_to_all(sent[1], 'ctx', split_axis=2, concat_axis=1, tiled=True)  5.09 us
    ppermute x3, starting transfers between devices, swapped_with_each(): lax.ppermute(sent, axis, [(i, i ^ step) for i in range(length)])  4.39 us
    dot_general x1, matrix products, segment_parts(): jnp.einsum('hqk,khd->qhd', probs_low, value_heads, preferred_element_type...  4.33 us
    gather x1, local copies, waits for them, and re-layouts, swapped_with_each(): parts = jnp.stack(done)[here ^ jnp.arange(length)]  3.56 us
  transfers between devices with their start and end apart: 5, of which 1 were waited for; matrix products, arithmetic and copies ran while one was open for 12% of the time, Pallas kernels for 0%

profile of v1, /device:TPU:0, one launch (start us, length us, event | category | flops | bytes accessed | tf_op | source)
XLA Modules:
  0.0 90.9 jit_solution(3181847861668207893)
XLA Ops:
  0.0 0.0 copy-start
  0.0 0.8 iota_compare_fusion
  0.9 0.9 and_reduce_fusion
  1.7 0.1 broadcast_bitcast_fusion
  1.8 0.2 copy.25
  2.0 0.0 copy-done
  2.0 0.0 copy-start.1
  2.1 5.3 %select_reduce_fusion = (f32[16,256]{1,0:T(8,128)S(1)}, f32[16,256,384]{2,1,0:T(8,128)}) fusion(pred[256,384]{1,0:T(8,128)(4,1)S(1)} %copy.25, bf16[384,2048]{1,0:T(8,128)(2,1)S(1)} %copy-done, bf16[256,2048]{1,0:T(8,128)(2,1)} %param.5), kind=kOutput, calls=%fused_computation.2 | convolution fusion | flops 407367680 | bytes 9027584 | tf_op jit(solution)/shard_map/qhd,khd->hqk/dot_general | solution.py:56
  7.4 0.6 broadcast_in_dim.48
  8.0 6.3 %all-to-all-start = ((f32[256,1,16]{0,1,2:T(1,128)}), f32[256,1,16]{0,1,2:T(1,128)S(1)}, u32[]{:S(2)}, u32[]{:S(2)}) async-start(f32[256,1,16]{0,1,2:T(1,128)} %broadcast_in_dim.48), calls=%async_computation | async-start | bytes 32768 | tf_op jit(solution)/shard_map/all_to_all | solution.py:93
  14.3 0.0 copy-done.1
  14.3 1.6 %copy.32 = bf16[384,2048]{0,1:T(8,128)(2,1)} copy(bf16[384,2048]{1,0:T(8,128)(2,1)S(1)} %copy-done.1) | data formatting | bytes 3145728 | tf_op jit(solution)/shard_map/reshape | solution.py:75
  15.9 0.0 slice-start
  15.9 0.0 slice-start.1
  15.9 4.3 %fusion.2 = f32[16,256,128]{1,2,0:T(8,128)S(1)} fusion(bf16[384,16,128]{0,2,1:T(8,128)(2,1)} %bitcast.71, f32[16,256,384]{2,1,0:T(8,128)} %get-tuple-element.12, f32[16,256]{1,0:T(8,128)S(1)} %get-tuple-element.11, pred[256,384]{1,0:T(8,128)(4,1)S(1)} %copy.25), kind=kOutput, calls=%fused_computation.5 | convolution fusion | flops 408944640 | bytes 10076160 | tf_op jit(solution)/shard_map/hqk,khd->qhd/dot_general | solution.py:63
  20.2 1.2 %dynamic-slice_bitcast_fusion.3 = (f32[1,256,1,512]{1,3,2,0:T(8,128)S(1)}, f32[256,1,512]{0,2,1:T(8,128)}, f32[256,1,512]{0,2,1:T(8,128)}, f32[256,1,512]{0,2,1:T(8,128)}) fusion(f32[256,1,4,512]{0,3,2,1:T(8,128)S(1)} %bitcast.70, s32[]{:T(128)S(6)} %select_n.31, s32[]{:T(128)S(6)} %select_n.34, s32[]{:T(128)S(6)} %select_n.33, s32[]{:T(128)S(6)} %select_n.32), kind=kLoop, calls=%fused_computation.23 | loop fusion | bytes 4194320 | tf_op jit(solution)/shard_map/dynamic_slice | solution.py:26
  21.4 3.8 %collective-permute-start.2 = (f32[256,1,512]{0,2,1:T(8,128)}, f32[256,1,512]{0,2,1:T(8,128)}, u32[]{:S(2)}, u32[]{:S(2)}) collective-permute-start(f32[256,1,512]{0,2,1:T(8,128)} %get-tuple-element.8), channel_id=1, source_target_pairs={{0,24},{8,16},{16,8},{24,0},{1,25},{9,17},{17,9},{25,1},{2,26},{10... | collective-permute-start | bytes 1572872 | tf_op jit(solution)/shard_map/ppermute | solution.py:29
  25.3 0.0 collective-permute-start.1
  25.3 0.6 collective-permute-start
  25.8 0.0 slice-done
  25.8 0.0 slice-done.1
  25.8 2.0 %fusion = f32[16,256]{1,0:T(8,128)S(1)} fusion(f32[16,256,384]{2,1,0:T(8,128)S(1)} %bitcast.69, f32[16,256]{1,0:T(8,128)S(1)} %get-tuple-element.11, pred[256,384]{1,0:T(8,128)(4,1)S(1)} %copy.25), kind=kLoop, calls=%fused_computation.3 | loop fusion | flops 6287360 | bytes 6422528 | tf_op jit(solution)/shard_map/reduce_sum | solution.py:61
  27.9 0.6 broadcast_in_dim.49
  28.5 0.0 all-to-all-done
  28.5 5.1 %all-to-all-start.1 = ((f32[256,1,16]{0,1,2:T(1,128)}), f32[256,1,16]{0,1,2:T(1,128)S(1)}, u32[]{:S(2)}, u32[]{:S(2)}) async-start(f32[256,1,16]{0,1,2:T(1,128)} %broadcast_in_dim.49), calls=%async_computation.1 | async-start | bytes 32768 | tf_op jit(solution)/shard_map/all_to_all | solution.py:94
  33.7 36.6 %all-to-all-done.1 = f32[256,1,16]{0,1,2:T(1,128)S(1)} async-done(((f32[256,1,16]{0,1,2:T(1,128)}), f32[256,1,16]{0,1,2:T(1,128)S(1)}, u32[]{:S(2)}, u32[]{:S(2)}) %all-to-all-start.1) | async-done | bytes 16416 | tf_op jit(solution)/shard_map/all_to_all | solution.py:94
  70.4 0.1 copy.30
  70.5 0.3 div.12
  70.9 0.2 div.13
  71.1 0.0 collective-permute-done.2
  71.1 0.0 collective-permute-done.1
  71.1 0.0 collective-permute-done
  71.1 2.9 %maximum_bitcast_fusion = f32[4,256,512]{1,2,0:T(8,128)} fusion(f32[1,256,1,512]{1,3,2,0:T(8,128)} %bitcast.12, f32[1,256,1,512]{1,3,2,0:T(8,128)} %bitcast.10, f32[1,256,1,512]{1,3,2,0:T(8,128)} %bitcast.8, f32[1,256,1,512]{1,3,2,0:T(8,128)S(1)} %get-tuple-element.7), kind=kLoop, calls=%fused_computation.10 | loop fusion | flops 1572864 | bytes 4194304 | tf_op jit(solution)/shard_map/stack | solution.py:30
  74.0 3.6 %gather_fusion = f32[4,256,512]{1,2,0:T(8,128)} fusion(f32[4,256,512]{1,2,0:T(8,128)} %maximum_bitcast_fusion, s32[1024]{0:T(1024)S(1)} %pad_clamp_fusion), kind=kCustom, calls=%fused_computation | custom fusion | bytes 4194320 | tf_op jit(solution)/shard_map/gather | solution.py:30
  77.6 1.8 %fusion.8 = f32[256,512]{0,1:T(8,128)S(1)} fusion(f32[4,256,512]{1,2,0:T(8,128)} %gather_fusion, f32[256,4,4]{0,2,1:T(4,128)S(1)} %get-tuple-element.6), kind=kLoop, calls=%fused_computation.12 | loop fusion | flops 917504 | bytes 2637824 | tf_op jit(solution)/shard_map/reduce_sum | solution.py:41
  79.4 0.2 copy.29
  79.6 0.1 fusion.14
  79.7 0.1 copy.31
  79.8 10.5 %all_to_all.39 = bf16[32,8,512]{2,0,1:T(8,128)(2,1)S(1)} all-to-all(bf16[32,8,512]{2,0,1:T(8,128)(2,1)S(1)} %copy.31), channel_id=1, replica_groups=mesh['ctx'=4,'row'=8] {'row'}, dimensions={1} | all-to-all | bytes 524288 | tf_op jit(solution)/shard_map/all_to_all | solution.py:102
  90.2 0.7 copy.50
  (11 shorter events, 0.2 us)
Async XLA Ops:
  0.0 2.0 %copy-start = (bf16[384,2048]{1,0:T(8,128)(2,1)S(1)}, bf16[384,2048]{1,0:T(8,128)(2,1)}, u32[]{:S(2)}) copy-start(bf16[384,2048]{1,0:T(8,128)(2,1)} %param.6) | copy-start | bytes 4718596
  2.0 12.3 %copy-start.1 = (bf16[384,2048]{1,0:T(8,128)(2,1)S(1)}, bf16[384,2048]{1,0:T(8,128)(2,1)}, u32[]{:S(2)}) copy-start(bf16[384,2048]{1,0:T(8,128)(2,1)} %param.7) | copy-start | bytes 4718596
  8.0 20.5 %all-to-all-start = ((f32[256,1,16]{0,1,2:T(1,128)}), f32[256,1,16]{0,1,2:T(1,128)S(1)}, u32[]{:S(2)}, u32[]{:S(2)}) async-start(f32[256,1,16]{0,1,2:T(1,128)} %broadcast_in_dim.48), calls=%async_computation | async-start | bytes 32768 | tf_op jit(solution)/shard_map/all_to_all | solution.py:93
  15.9 10.0 %slice-start = ((s8[6291456]{0:T(1024)(128)(4,1)}), s8[4194304]{0:T(1024)(128)(4,1)S(1)}, s32[]{:S(2)}) async-start(s8[6291456]{0:T(1024)(128)(4,1)} %bitcast.68), calls=%async_computation.3 | async-start | bytes 8388608
  15.9 10.0 %slice-start.1 = ((s8[6291456]{0:T(1024)(128)(4,1)}), s8[2097152]{0:T(1024)(128)(4,1)S(1)}, s32[]{:S(2)}) async-start(s8[6291456]{0:T(1024)(128)(4,1)} %bitcast.68), calls=%async_computation.4 | async-start | bytes 4194304
  21.4 49.7 %collective-permute-start.2 = (f32[256,1,512]{0,2,1:T(8,128)}, f32[256,1,512]{0,2,1:T(8,128)}, u32[]{:S(2)}, u32[]{:S(2)}) collective-permute-start(f32[256,1,512]{0,2,1:T(8,128)} %get-tuple-element.8), channel_id=1, source_target_pairs={{0,24},{8,16},{16,8},{24,0},{1,25},{9,17},{17,9},{25,1},{2,26},{10... | collective-permute-start | bytes 1572872 | tf_op jit(solution)/shard_map/ppermute | solution.py:29
  25.3 45.8 %collective-permute-start.1 = (f32[256,1,512]{0,2,1:T(8,128)}, f32[256,1,512]{0,2,1:T(8,128)}, u32[]{:S(2)}, u32[]{:S(2)}) collective-permute-start(f32[256,1,512]{0,2,1:T(8,128)} %get-tuple-element.9), channel_id=1, source_target_pairs={{0,16},{8,24},{16,0},{24,8},{1,17},{9,25},{17,1},{25,9},{2,18},{10... | collective-permute-start | bytes 1572872 | tf_op jit(solution)/shard_map/ppermute | solution.py:29
  25.3 45.9 %collective-permute-start = (f32[256,1,512]{0,2,1:T(8,128)}, f32[256,1,512]{0,2,1:T(8,128)}, u32[]{:S(2)}, u32[]{:S(2)}) collective-permute-start(f32[256,1,512]{0,2,1:T(8,128)} %get-tuple-element.10), channel_id=1, source_target_pairs={{0,8},{8,0},{16,24},{24,16},{1,9},{9,1},{17,25},{25,17},{2,10},{10... | collective-permute-start | bytes 1572872 | tf_op jit(solution)/shard_map/ppermute | solution.py:29
  28.5 41.8 %all-to-all-start.1 = ((f32[256,1,16]{0,1,2:T(1,128)}), f32[256,1,16]{0,1,2:T(1,128)S(1)}, u32[]{:S(2)}, u32[]{:S(2)}) async-start(f32[256,1,16]{0,1,2:T(1,128)} %broadcast_in_dim.49), calls=%async_computation.1 | async-start | bytes 32768 | tf_op jit(solution)/shard_map/all_to_all | solution.py:94
